TPU v7x, 32 devices: a whole 2x2x4 slice. The times are simulated.
32 devices in a mesh: slab: 2 (over y), frame: 4 (over z), coil: 4 (over x, core).
Axes of the slice: x: 2, y: 2, z: 4, core: 2. Of those that a mesh axis runs over, the one named last changes fastest.
Arguments:
- factors: float32 [4, 16, 256, 256], P('slab', None, 'coil', 'frame'), parts along dimension 0, may hold values from -3 to 3
- temporal: float32 [4, 4, 16], P('slab'), parts along dimension 0, may hold values from -3 to 3
- maps: bfloat16 [32, 512, 512], P('coil', 'slab'), parts along dimension 1, may hold values from -1 to 1
- kdata: bfloat16 [4, 32, 512, 512], P('frame', 'coil', 'slab'), parts along dimension 2, may hold values from -1.5 to 1.5
- masks: int32 [4, 32, 512], P('frame', 'coil', 'slab'), parts along dimension 2, may hold values 0 or 1
Outputs:
- new_factors: float32 [4, 16, 256, 256], P('slab', None, 'coil', 'frame'), parts along dimension 0
There are 2 independent parts, one for each index of `slab`. A program takes and returns all parts, laid end to end along the dimension named above; each array names one. Nothing has to cross between parts.
All inputs are finite; a program needn't handle non-finite values. No bound on the sum of `masks` on one device may be relied on, other than what follows from the above.
Results may differ from a plain program's by a relative error of at most 0.0085.
Values may be sent and summed in bfloat16 or wider, within the bound.
No kernel may reach another device: no remote copies, remote signals or barrier semaphores. Data moves between devices by JAX's collectives and lax.ppermute only.
A program may use at most 64 MiB of HBM per device.

v0:
```python
import math
import jax
import jax.numpy as jnp
from jax import lax
from jax.sharding import PartitionSpec as P


def dft_parts(length):
    index = jnp.arange(length, dtype=jnp.int32)
    phase = index[:, None] * index[None, :] % length
    angle = 2.0 * math.pi / length * phase.astype(jnp.float32)
    scale = 1.0 / math.sqrt(length)
    return (
        (jnp.cos(angle) * scale).astype(jnp.bfloat16),
        (-jnp.sin(angle) * scale).astype(jnp.bfloat16),
    )


def rotate_plus(values, half_width):
    return jnp.concatenate([-values[..., half_width:], values[..., :half_width]], axis=-1)


def rotate_minus(values, half_width):
    return jnp.concatenate([values[..., half_width:], -values[..., :half_width]], axis=-1)


def sens_times(sens, values, half_width):
    sens_re = sens[..., :half_width].astype(jnp.float32)
    sens_im = sens[..., half_width:].astype(jnp.float32)
    value_re = values[..., :half_width].astype(jnp.float32)
    value_im = values[..., half_width:].astype(jnp.float32)
    return jnp.concatenate(
        [sens_re * value_re - sens_im * value_im, sens_re * value_im + sens_im * value_re], axis=-1
    )


def conj_sens_times(sens, values, half_width):
    sens_re = sens[..., :half_width].astype(jnp.float32)
    sens_im = sens[..., half_width:].astype(jnp.float32)
    value_re = values[..., :half_width]
    value_im = values[..., half_width:]
    return jnp.concatenate(
        [sens_re * value_re + sens_im * value_im, sens_re * value_im - sens_im * value_re], axis=-1
    )


def precise(form, first, second):
    return jnp.einsum(form, first, second, precision=lax.Precision.HIGHEST)


def on_device(factors, temporal, maps, kdata, masks):
    width_x = maps.shape[2] // 2
    width_y = maps.shape[1]
    rows_own = factors.shape[2]
    table_x_re, table_x_im = dft_parts(width_x)
    table_y_re, table_y_im = dft_parts(width_y)
    forward_x = jnp.concatenate(
        [
            jnp.concatenate([table_x_re, table_x_im], axis=1),
            jnp.concatenate([-table_x_im, table_x_re], axis=1),
        ],
        axis=0,
    )
    adjoint_x = jnp.concatenate(
        [
            jnp.concatenate([table_x_re, -table_x_im], axis=1),
            jnp.concatenate([table_x_im, table_x_re], axis=1),
        ],
        axis=0,
    )
    wide_y = jnp.concatenate([table_y_re, table_y_im], axis=1)
    left_re = factors[0]
    left_im = factors[1]
    time_re = temporal[0]
    time_im = temporal[1]
    image_re = precise("tr,ryx->tyx", time_re, left_re) - precise("tr,ryx->tyx", time_im, left_im)
    image_im = precise("tr,ryx->tyx", time_im, left_re) + precise("tr,ryx->tyx", time_re, left_im)
    images = jnp.stack([image_re, image_im], axis=2).astype(jnp.bfloat16)
    own_frame = lax.all_to_all(images, "frame", split_axis=0, concat_axis=3, tiled=True)
    own_rows = own_frame.reshape(own_frame.shape[1], 2 * width_x)
    sens = maps
    coil_image = sens_times(
        sens, lax.all_gather(own_rows, "coil", axis=0, tiled=True)[None], width_x
    ).astype(jnp.bfloat16)
    half_k = jnp.einsum(
        "cyn,nm->cym", coil_image, forward_x, preferred_element_type=jnp.float32
    ).astype(jnp.bfloat16)
    stacked = jnp.concatenate([half_k, rotate_plus(half_k, width_x)], axis=1)
    kspace = jnp.einsum("kj,cjn->ckn", wide_y, stacked, preferred_element_type=jnp.float32)
    sampled = masks[0].astype(jnp.float32)[:, :, None]
    residual = (sampled * (kspace - kdata[0].astype(jnp.float32))).astype(jnp.bfloat16)
    resid_stack = jnp.concatenate([residual, rotate_minus(residual, width_x)], axis=1)
    back_half = jnp.einsum(
        "kj,cjn->ckn", wide_y, resid_stack, preferred_element_type=jnp.float32
    ).astype(jnp.bfloat16)
    coil_back = jnp.einsum("cyn,nm->cym", back_half, adjoint_x, preferred_element_type=jnp.float32)
    sens = maps
    combined = lax.psum(
        jnp.sum(conj_sens_times(sens, coil_back, width_x), axis=0).astype(jnp.bfloat16), "coil"
    ).astype(jnp.float32)
    own_share = lax.dynamic_slice_in_dim(combined, lax.axis_index("coil") * rows_own, rows_own, 0)
    returned = lax.all_to_all(
        own_share.reshape(1, rows_own, 2, width_x).astype(jnp.bfloat16),
        "frame",
        split_axis=3,
        concat_axis=0,
        tiled=True,
    ).astype(jnp.float32)
    back_re = returned[:, :, 0]
    back_im = returned[:, :, 1]
    grad_re = precise("tr,tyx->ryx", time_re, back_re) + precise("tr,tyx->ryx", time_im, back_im)
    grad_im = precise("tr,tyx->ryx", time_re, back_im) - precise("tr,tyx->ryx", time_im, back_re)
    return factors - 0.5 * jnp.stack([grad_re, grad_im])


def solution(mesh):
    placed = (
        P("slab", None, "coil", "frame"),
        P("slab", None, None),
        P("coil", "slab", None),
        P("frame", "coil", "slab", None),
        P("frame", "coil", "slab"),
    )
    return jax.shard_map(
        on_device,
        mesh=mesh,
        in_specs=placed,
        out_specs=P("slab", None, "coil", "frame"),
        check_vma=False,
    )
```

profile of v0, /device:TPU:0, one launch (start us, length us, event | category | flops | bytes accessed | tf_op | source)
XLA Modules:
  0.0 103.2 jit_solution(2421429024773020784)
XLA Ops:
  6.5 1.8 %copy.40 = f32[2,16,64,64]{3,1,2,0:T(8,128)S(1)} copy(f32[2,16,64,64]{3,2,1,0:T(8,128)} %param.5) | data formatting | bytes 1048576 | tf_op args[0]
  10.1 0.8 reshape.35
  10.9 6.3 %all-to-all-start = ((bf16[4,2,4096]{2,1,0:T(2,128)(2,1)}), bf16[4,2,4096]{2,1,0:T(2,128)(2,1)S(1)}, u32[]{:S(2)}, u32[]{:S(2)}) async-start(bf16[4,2,4096]{2,1,0:T(2,128)(2,1)} %reshape.35), calls=%async_computation | async-start | bytes 131072 | tf_op jit(solution)/shard_map/all_to_all | solution.py:79
  17.2 1.1 %multiply_convert_fusion = (bf16[256,256]{1,0:T(8,128)(2,1)S(1)}, bf16[256,256]{1,0:T(8,128)(2,1)S(1)}) fusion(), kind=kLoop, calls=%fused_computation.75 | loop fusion | flops 1245184 | bytes 262144 | tf_op jit(solution)/shard_map/convert_element_type | solution.py:15
  18.4 2.4 %copy.36 = bf16[1,8,256,512]{2,3,1,0:T(8,128)(2,1)} copy(bf16[1,8,256,512]{3,2,1,0:T(8,128)(2,1)S(1)} %copy-done.2) | data formatting | bytes 4194304 | tf_op args[3]
  20.8 1.0 fusion.65
  21.8 1.2 %all-to-all-done = bf16[4,2,4096]{2,1,0:T(2,128)(2,1)S(1)} async-done(((bf16[4,2,4096]{2,1,0:T(2,128)(2,1)}), bf16[4,2,4096]{2,1,0:T(2,128)(2,1)S(1)}, u32[]{:S(2)}, u32[]{:S(2)}) %all-to-all-start) | async-done | bytes 65568 | tf_op jit(solution)/shard_map/all_to_all | solution.py:79
  23.4 6.0 %all_gather.3 = bf16[256,512]{1,0:T(8,128)(2,1)S(1)} all-gather(bf16[64,512]{1,0:T(8,128)(2,1)S(1)} %reshape.26), channel_id=1, replica_groups=mesh['slab'=2,'frame'=4,'coil'=4] {'coil'}, dimensions={0}, use_global_device_ids=true | all-gather | bytes 327680 | tf_op jit(solution)/shard_map/all_gather | solution.py:83
  29.4 0.8 fusion.17
  30.2 1.3 %fusion.29 = bf16[8,256,512]{2,1,0:T(8,128)(2,1)S(1)} fusion(bf16[8,256,256]{2,1,0:T(8,128)(2,1)S(1)} %get-tuple-element.8, bf16[8,256,256]{2,1,0:T(8,128)(2,1)S(1)} %get-tuple-element.7, bf16[256,256]{1,0:T(8,128)(2,1)S(1)} %get-tuple-element.16, bf16[256,256]{1,0:T(8,128)(2,1)S(1)} %fusion.65, bf16[256,256]{1,0:T(8,128)(2,1)S(1)} %get-tuple-element.15), kind=kOutput, calls=%fused_computation.37 | convolution fusion | flops 1081081856 | bytes 4587520 | tf_op jit(solution)/shard_map/cyn,nm->cym/dot_general | solution.py:85
  31.6 1.4 %copy-done.3 = bf16[1,8,256,512]{2,3,1,0:T(8,128)(2,1)S(1)} copy-done((bf16[1,8,256,512]{2,3,1,0:T(8,128)(2,1)S(1)}, bf16[1,8,256,512]{2,3,1,0:T(8,128)(2,1)}, u32[]{:S(2)}) %copy-start.3) | copy-done | bytes 2097176
  33.1 1.6 %fusion.13 = bf16[8,256,512]{1,2,0:T(8,128)(2,1)S(1)} fusion(bf16[8,256,256]{2,1,0:T(8,128)(2,1)S(1)} %get-tuple-element.12, bf16[8,256,256]{2,1,0:T(8,128)(2,1)S(1)} %get-tuple-element.11, bf16[8,256,512]{2,1,0:T(8,128)(2,1)S(1)} %fusion.29, bf16[1,8,256,512]{2,3,1,0:T(8,128)(2,1)S(1)} %copy-done.3, f32[8,256]{1,0:T(8,128)S(1)} %convert_bitcast_fusion, ...), kind=kOutput, calls=%fused_computation.15 | convolution fusion | flops 1091043328 | bytes 8658944 | tf_op jit(solution)/shard_map/kj,cjn->ckn/dot_general | solution.py:89
  34.6 1.2 %fusion.86 = (bf16[8,256,256]{1,2,0:T(8,128)(2,1)S(1)}, bf16[8,256,256]{1,2,0:T(8,128)(2,1)}) fusion(bf16[8,256,512]{1,2,0:T(8,128)(2,1)S(1)} %fusion.13), kind=kLoop, calls=%fused_computation.111 | loop fusion | flops 524288 | bytes 4194304 | tf_op jit(solution)/shard_map/slice | solution.py:24
  36.3 8.3 %fusion.26 = f32[8,256,512]{2,1,0:T(8,128)} fusion(bf16[8,256,256]{1,2,0:T(8,128)(2,1)} %get-tuple-element.10, bf16[8,256,256]{1,2,0:T(8,128)(2,1)S(1)} %get-tuple-element.9, bf16[8,256,512]{1,2,0:T(8,128)(2,1)} %copy-done.4, bf16[256,256]{1,0:T(8,128)(2,1)S(1)} %get-tuple-element.16, bf16[256,256]{1,0:T(8,128)(2,1)S(1)} %get-tuple-element.15, ...), kind=kOutput, calls=%fused_computation.34 | convolution fusion | flops 2163736576 | bytes 8781824 | tf_op jit(solution)/shard_map/cyn,nm->cym/dot_general | solution.py:96
  44.6 2.9 %fusion.20 = (f32[8,256,256]{2,1,0:T(8,128)S(1)}, f32[8,256,256]{2,1,0:T(8,128)S(1)}) fusion(f32[8,256,512]{2,1,0:T(8,128)} %fusion.26, bf16[8,256,512]{2,1,0:T(8,128)(2,1)S(1)} %copy-done), kind=kLoop, calls=%fused_computation.28 | loop fusion | flops 4194304 | bytes 10485760 | tf_op jit(solution)/shard_map/add | solution.py:43
  47.5 1.0 maximum_reduce_fusion
  48.5 32.4 %all-reduce.2.cloned.1.call-done = bf16[256,512]{1,0:T(8,128)(2,1)} async-done(((bf16[256,512]{1,0:T(8,128)(2,1)}), bf16[256,512]{1,0:T(8,128)(2,1)}) %all-reduce.2.cloned.1.call-update) | async-done | bytes 262160 | tf_op jit(solution)/shard_map/psum | solution.py:98
  80.9 0.8 convert_convert_fusion
  82.1 10.3 %all_to_all.33 = bf16[4,2,4096]{2,1,0:T(2,128)(2,1)S(1)} all-to-all(bf16[4,2,4096]{2,1,0:T(2,128)(2,1)S(1)} %reshape.37), channel_id=1, replica_groups=mesh['slab'=2,'frame'=4,'coil'=4] {'frame'}, dimensions={0} | all-to-all | bytes 131072 | tf_op jit(solution)/shard_map/all_to_all | solution.py:102
  92.7 0.4 fusion.63
  93.5 0.4 fusion.37
  94.0 0.4 fusion.36
  94.4 0.7 fusion.42
  95.1 1.3 %copy.41 = f32[2,16,64,64]{3,2,1,0:T(8,128)} copy(f32[2,16,64,64]{3,1,2,0:T(8,128)S(1)} %fusion.42) | data formatting | bytes 1048576 | tf_op jit(solution)/shard_map/sub | solution.py:113
  (34 shorter events, 3.7 us)
Async XLA Ops:
  6.5 1.9 %copy-start.5 = (f32[2,4,16]{2,1,0:T(4,128)S(1)}, f32[2,4,16]{2,1,0:T(4,128)}, u32[]{:S(2)}) copy-start(f32[2,4,16]{2,1,0:T(4,128)} %param.6) | copy-start | bytes 1540
  8.4 9.9 %copy-start.2 = (bf16[1,8,256,512]{3,2,1,0:T(8,128)(2,1)S(1)}, bf16[1,8,256,512]{3,2,1,0:T(8,128)(2,1)}, u32[]{:S(2)}) copy-start(bf16[1,8,256,512]{3,2,1,0:T(8,128)(2,1)} %param.8) | copy-start | bytes 6291460
  10.9 12.1 %all-to-all-start = ((bf16[4,2,4096]{2,1,0:T(2,128)(2,1)}), bf16[4,2,4096]{2,1,0:T(2,128)(2,1)S(1)}, u32[]{:S(2)}, u32[]{:S(2)}) async-start(bf16[4,2,4096]{2,1,0:T(2,128)(2,1)} %reshape.35), calls=%async_computation | async-start | bytes 131072 | tf_op jit(solution)/shard_map/all_to_all | solution.py:79
  17.2 63.7 %all-reduce.2.cloned.1.call-start = ((), (), s32[]{:S(2)}) async-start(), calls=%async_computation.2 | async-start | bytes 524288 | tf_op jit(solution)/shard_map/psum | solution.py:98
  18.3 2.4 %copy-start.6 = (s32[1,8,256]{2,1,0:T(8,128)S(1)}, s32[1,8,256]{2,1,0:T(8,128)}, u32[]{:S(2)}) copy-start(s32[1,8,256]{2,1,0:T(8,128)} %param.9) | copy-start | bytes 24580
  20.8 8.6 %copy-start = (bf16[8,256,512]{2,1,0:T(8,128)(2,1)S(1)}, bf16[8,256,512]{2,1,0:T(8,128)(2,1)}, u32[]{:S(2)}) copy-start(bf16[8,256,512]{2,1,0:T(8,128)(2,1)} %param.7) | copy-start | bytes 6291460
  31.5 1.6 %copy-start.3 = (bf16[1,8,256,512]{2,3,1,0:T(8,128)(2,1)S(1)}, bf16[1,8,256,512]{2,3,1,0:T(8,128)(2,1)}, u32[]{:S(2)}) copy-start(bf16[1,8,256,512]{2,3,1,0:T(8,128)(2,1)} %copy.36) | copy-start | bytes 6291460
  34.6 1.6 %copy-start.4 = (bf16[8,256,512]{1,2,0:T(8,128)(2,1)}, bf16[8,256,512]{1,2,0:T(8,128)(2,1)S(1)}, u32[]{:S(2)}) copy-start(bf16[8,256,512]{1,2,0:T(8,128)(2,1)S(1)} %fusion.13) | copy-start | bytes 6291460
  81.9 12.5 %copy-start.1 = (f32[2,16,64,64]{3,2,1,0:T(8,128)S(1)}, f32[2,16,64,64]{3,2,1,0:T(8,128)}, u32[]{:S(2)}) copy-start(f32[2,16,64,64]{3,2,1,0:T(8,128)} %param.5) | copy-start | bytes 1572868
Sparse Core Ops, SparseCore 0:
  48.6 32.2 all-reduce.1
where the time goes:
time: 104 us; the launch traced here: 103 us
  waiting for transfers between devices  33.6 us (32%)
  blocking collectives  16.2 us (16%)
  matrix products  14.3 us (14%)
  between operations  13.7 us (13%)
  other arithmetic  9.76 us (9%)
  local copies, waits for them, and re-layouts  9.24 us (9%)
  starting transfers between devices  6.32 us (6%)
    psum x1, waiting for transfers between devices, on_device(): lax.psum(jnp.sum(conj_sens_times(sens, coil_back, width_x), axis=0).astyp...  32.4 us
    all_to_all x1, blocking collectives, on_device(): lax.all_to_all(own_share.reshape(1, rows_own, 2, width_x).astype(jnp.bflo...  10.3 us
    dot_general x1, matrix products, on_device(): jnp.einsum('cyn,nm->cym', back_half, adjoint_x, preferred_element_type=jn...  8.28 us
    unnamed x20, local copies, waits for them, and re-layouts  7.37 us
    all_to_all x1, starting transfers between devices, on_device(): lax.all_to_all(images, 'frame', split_axis=0, concat_axis=3, tiled=True)  6.32 us
    all_gather x1, blocking collectives, on_device(): lax.all_gather(own_rows, 'coil', axis=0, tiled=True)[None]  5.97 us
    dot_general x8, matrix products, precise(): return jnp.einsum(form, first, second, precision=lax.Precision.HIGHEST)  3.21 us
    add x1, other arithmetic, conj_sens_times(): sens_re * value_re + sens_im * value_im  2.93 us
  transfers between devices with their start and end apart: 2, of which 2 were waited for; matrix products, arithmetic and copies ran while one was open for 4% of the time, Pallas kernels for 0%

commit v1 on v0

--- a/solution.py
+++ b/solution.py
@@ -95,8 +95,11 @@
     ).astype(jnp.bfloat16)
     coil_back = jnp.einsum("cyn,nm->cym", back_half, adjoint_x, preferred_element_type=jnp.float32)
     sens = maps
-    combined = lax.psum(
-        jnp.sum(conj_sens_times(sens, coil_back, width_x), axis=0).astype(jnp.bfloat16), "coil"
+    combined = jnp.sum(
+        lax.all_gather(
+            jnp.sum(conj_sens_times(sens, coil_back, width_x), axis=0).astype(jnp.bfloat16), "coil"
+        ),
+        axis=0,
     ).astype(jnp.float32)
     own_share = lax.dynamic_slice_in_dim(combined, lax.axis_index("coil") * rows_own, rows_own, 0)
     returned = lax.all_to_all(

time: 104 us -> 88.8 us (0.85)
  waiting for transfers between devices: 33.6 us -> 18.4 us
    psum x1 -> x0, waiting for transfers between devices: 32.4 us -> none  [on_device(): lax.psum(jnp.sum(conj_sens_times(sens, coil_back, width_x), axis=0).astyp...]
    all_gather x0 -> x1, waiting for transfers between devices: none -> 17.2 us  [on_device(): lax.all_gather(jnp.sum(conj_sens_times(sens, coil_back, width_x), axis=0)...]
    reduce_sum x0 -> x1, other arithmetic: none -> 1.45 us  [on_device(): jnp.sum(lax.all_gather(jnp.sum(conj_sens_times(sens, coil_back, width_x),...]
  transfers between devices with their start and end apart: 2 -> 2, of which waited for: 2 -> 2; matrix products, arithmetic and copies ran while one was open for 4% -> 5% of each run, Pallas kernels for 0% -> 0%
where the time goes in v1:
time: 88.8 us; the launch traced here: 88.5 us
  waiting for transfers between devices  18.4 us (21%)
  blocking collectives  16.2 us (18%)
  matrix products  14.3 us (16%)
  between operations  13.7 us (15%)
  other arithmetic  10.3 us (12%)
  local copies, waits for them, and re-layouts  9.24 us (10%)
  starting transfers between devices  6.32 us (7%)
    all_gather x1, waiting for transfers between devices, on_device(): lax.all_gather(jnp.sum(conj_sens_times(sens, coil_back, width_x), axis=0)...  17.2 us
    all_to_all x1, blocking collectives, on_device(): lax.all_to_all(own_share.reshape(1, rows_own, 2, width_x).astype(jnp.bflo...  10.3 us
    dot_general x1, matrix products, on_device(): jnp.einsum('cyn,nm->cym', back_half, adjoint_x, preferred_element_type=jn...  8.27 us
    unnamed x20, local copies, waits for them, and re-layouts  7.37 us
    all_to_all x1, starting transfers between devices, on_device(): lax.all_to_all(images, 'frame', split_axis=0, concat_axis=3, tiled=True)  6.32 us
    all_gather x1, blocking collectives, on_device(): lax.all_gather(own_rows, 'coil', axis=0, tiled=True)[None]  5.97 us
    dot_general x8, matrix products, precise(): return jnp.einsum(form, first, second, precision=lax.Precision.HIGHEST)  3.2 us
    add x1, other arithmetic, conj_sens_times(): sens_re * value_re + sens_im * value_im  2.83 us
  transfers between devices with their start and end apart: 2, of which 2 were waited for; matrix products, arithmetic and copies ran while one was open for 5% of the time, Pallas kernels for 0%

profile of v1, /device:TPU:0, one launch (start us, length us, event | category | flops | bytes accessed | tf_op | source)
XLA Modules:
  0.0 88.5 jit_solution(9057206702237832735)
XLA Ops:
  6.5 1.8 %copy.51 = f32[2,16,64,64]{3,1,2,0:T(8,128)S(1)} copy(f32[2,16,64,64]{3,2,1,0:T(8,128)} %param.5) | data formatting | bytes 1048576 | tf_op args[0]
  10.1 0.8 reshape.44
  10.9 6.3 %all-to-all-start = ((bf16[4,2,4096]{2,1,0:T(2,128)(2,1)}), bf16[4,2,4096]{2,1,0:T(2,128)(2,1)S(1)}, u32[]{:S(2)}, u32[]{:S(2)}) async-start(bf16[4,2,4096]{2,1,0:T(2,128)(2,1)} %reshape.44), calls=%async_computation | async-start | bytes 131072 | tf_op jit(solution)/shard_map/all_to_all | solution.py:79
  17.2 1.1 %multiply_convert_fusion = (bf16[256,256]{1,0:T(8,128)(2,1)S(1)}, bf16[256,256]{1,0:T(8,128)(2,1)S(1)}) fusion(), kind=kLoop, calls=%fused_computation.75 | loop fusion | flops 1245184 | bytes 262144 | tf_op jit(solution)/shard_map/convert_element_type | solution.py:15
  18.4 2.4 %copy.47 = bf16[1,8,256,512]{2,3,1,0:T(8,128)(2,1)} copy(bf16[1,8,256,512]{3,2,1,0:T(8,128)(2,1)S(1)} %copy-done.2) | data formatting | bytes 4194304 | tf_op args[3]
  20.8 1.0 %fusion.65 = bf16[256,256]{1,0:T(8,128)(2,1)S(1)} fusion(), kind=kLoop, calls=%fused_computation.90 | loop fusion | flops 1310720 | bytes 131072 | tf_op jit(solution)/shard_map/neg | solution.py:60
  21.8 1.2 %all-to-all-done = bf16[4,2,4096]{2,1,0:T(2,128)(2,1)S(1)} async-done(((bf16[4,2,4096]{2,1,0:T(2,128)(2,1)}), bf16[4,2,4096]{2,1,0:T(2,128)(2,1)S(1)}, u32[]{:S(2)}, u32[]{:S(2)}) %all-to-all-start) | async-done | bytes 65568 | tf_op jit(solution)/shard_map/all_to_all | solution.py:79
  23.4 6.0 %all_gather.7 = bf16[256,512]{1,0:T(8,128)(2,1)S(1)} all-gather(bf16[64,512]{1,0:T(8,128)(2,1)S(1)} %reshape.34), channel_id=1, replica_groups=mesh['slab'=2,'frame'=4,'coil'=4] {'coil'}, dimensions={0}, use_global_device_ids=true | all-gather | bytes 327680 | tf_op jit(solution)/shard_map/all_gather | solution.py:83
  29.4 0.7 fusion.17
  30.1 1.3 %fusion.29 = bf16[8,256,512]{2,1,0:T(8,128)(2,1)S(1)} fusion(bf16[8,256,256]{2,1,0:T(8,128)(2,1)S(1)} %get-tuple-element.8, bf16[8,256,256]{2,1,0:T(8,128)(2,1)S(1)} %get-tuple-element.7, bf16[256,256]{1,0:T(8,128)(2,1)S(1)} %get-tuple-element.16, bf16[256,256]{1,0:T(8,128)(2,1)S(1)} %fusion.65, bf16[256,256]{1,0:T(8,128)(2,1)S(1)} %get-tuple-element.15), kind=kOutput, calls=%fused_computation.37 | convolution fusion | flops 1081081856 | bytes 4587520 | tf_op jit(solution)/shard_map/cyn,nm->cym/dot_general | solution.py:85
  31.6 1.4 %copy-done.3 = bf16[1,8,256,512]{2,3,1,0:T(8,128)(2,1)S(1)} copy-done((bf16[1,8,256,512]{2,3,1,0:T(8,128)(2,1)S(1)}, bf16[1,8,256,512]{2,3,1,0:T(8,128)(2,1)}, u32[]{:S(2)}) %copy-start.3) | copy-done | bytes 2097176
  33.0 1.6 %fusion.13 = bf16[8,256,512]{1,2,0:T(8,128)(2,1)S(1)} fusion(bf16[8,256,256]{2,1,0:T(8,128)(2,1)S(1)} %get-tuple-element.12, bf16[8,256,256]{2,1,0:T(8,128)(2,1)S(1)} %get-tuple-element.11, bf16[8,256,512]{2,1,0:T(8,128)(2,1)S(1)} %fusion.29, bf16[1,8,256,512]{2,3,1,0:T(8,128)(2,1)S(1)} %copy-done.3, f32[8,256]{1,0:T(8,128)S(1)} %convert_bitcast_fusion, ...), kind=kOutput, calls=%fused_computation.15 | convolution fusion | flops 1091043328 | bytes 8658944 | tf_op jit(solution)/shard_map/kj,cjn->ckn/dot_general | solution.py:89
  34.6 1.2 %fusion.86 = (bf16[8,256,256]{1,2,0:T(8,128)(2,1)S(1)}, bf16[8,256,256]{1,2,0:T(8,128)(2,1)}) fusion(bf16[8,256,512]{1,2,0:T(8,128)(2,1)S(1)} %fusion.13), kind=kLoop, calls=%fused_computation.111 | loop fusion | flops 524288 | bytes 4194304 | tf_op jit(solution)/shard_map/slice | solution.py:24
  36.2 8.3 %fusion.26 = f32[8,256,512]{2,1,0:T(8,128)} fusion(bf16[8,256,256]{1,2,0:T(8,128)(2,1)} %get-tuple-element.10, bf16[8,256,256]{1,2,0:T(8,128)(2,1)S(1)} %get-tuple-element.9, bf16[8,256,512]{1,2,0:T(8,128)(2,1)} %copy-done.4, bf16[256,256]{1,0:T(8,128)(2,1)S(1)} %get-tuple-element.16, bf16[256,256]{1,0:T(8,128)(2,1)S(1)} %get-tuple-element.15, ...), kind=kOutput, calls=%fused_computation.34 | convolution fusion | flops 2163736576 | bytes 8781824 | tf_op jit(solution)/shard_map/cyn,nm->cym/dot_general | solution.py:96
  44.5 2.8 %fusion.20 = (f32[8,256,256]{2,1,0:T(8,128)S(1)}, f32[8,256,256]{2,1,0:T(8,128)S(1)}) fusion(f32[8,256,512]{2,1,0:T(8,128)} %fusion.26, bf16[8,256,512]{2,1,0:T(8,128)(2,1)S(1)} %copy-done), kind=kLoop, calls=%fused_computation.28 | loop fusion | flops 4194304 | bytes 10485760 | tf_op jit(solution)/shard_map/add | solution.py:43
  47.3 1.0 %maximum_reduce_fusion = bf16[256,512]{1,0:T(8,128)(2,1)} fusion(f32[8,256,256]{2,1,0:T(8,128)S(1)} %get-tuple-element.6, f32[8,256,256]{2,1,0:T(8,128)S(1)} %get-tuple-element.5), kind=kLoop, calls=%fused_computation.12 | loop fusion | flops 1966080 | bytes 4456448 | tf_op jit(solution)/shard_map/reduce_sum | solution.py:100
  48.3 17.2 %all-gather.3.cloned.1.call-done = bf16[1024,512]{1,0:T(8,128)(2,1)} async-done(((bf16[256,512]{1,0:T(8,128)(2,1)}), bf16[1024,512]{1,0:T(8,128)(2,1)}) %all-gather.3.cloned.1.call-update) | async-done | bytes 1048592 | tf_op jit(solution)/shard_map/all_gather | solution.py:99
  65.5 1.5 %reduce_sum.22 = bf16[256,512]{1,0:T(8,128)(2,1)S(1)} reduce(bf16[4,256,512]{2,1,0:T(8,128)(2,1)} %bitcast.101, bf16[]{:T(256)} %constant.31.clone.1), dimensions={0}, to_apply=%region_1.2 | reduce | flops 393216 | bytes 1310722 | tf_op jit(solution)/shard_map/reduce_sum | solution.py:98
  67.3 10.3 %all_to_all.33 = bf16[4,2,4096]{2,1,0:T(2,128)(2,1)S(1)} all-to-all(bf16[4,2,4096]{2,1,0:T(2,128)(2,1)S(1)} %reshape.46), channel_id=1, replica_groups=mesh['slab'=2,'frame'=4,'coil'=4] {'frame'}, dimensions={0} | all-to-all | bytes 131072 | tf_op jit(solution)/shard_map/all_to_all | solution.py:105
  77.9 0.4 fusion.63
  78.8 0.4 fusion.37
  79.2 0.4 fusion.36
  79.7 0.7 fusion.42
  80.3 1.3 %copy.52 = f32[2,16,64,64]{3,2,1,0:T(8,128)} copy(f32[2,16,64,64]{3,1,2,0:T(8,128)S(1)} %fusion.42) | data formatting | bytes 1048576 | tf_op jit(solution)/shard_map/sub | solution.py:116
  (35 shorter events, 3.7 us)
Async XLA Ops:
  6.5 1.9 %copy-start.5 = (f32[2,4,16]{2,1,0:T(4,128)S(1)}, f32[2,4,16]{2,1,0:T(4,128)}, u32[]{:S(2)}) copy-start(f32[2,4,16]{2,1,0:T(4,128)} %param.6) | copy-start | bytes 1540
  8.4 9.9 %copy-start.2 = (bf16[1,8,256,512]{3,2,1,0:T(8,128)(2,1)S(1)}, bf16[1,8,256,512]{3,2,1,0:T(8,128)(2,1)}, u32[]{:S(2)}) copy-start(bf16[1,8,256,512]{3,2,1,0:T(8,128)(2,1)} %param.8) | copy-start | bytes 6291460
  10.9 12.1 %all-to-all-start = ((bf16[4,2,4096]{2,1,0:T(2,128)(2,1)}), bf16[4,2,4096]{2,1,0:T(2,128)(2,1)S(1)}, u32[]{:S(2)}, u32[]{:S(2)}) async-start(bf16[4,2,4096]{2,1,0:T(2,128)(2,1)} %reshape.44), calls=%async_computation | async-start | bytes 131072 | tf_op jit(solution)/shard_map/all_to_all | solution.py:79
  17.2 48.3 %all-gather.3.cloned.1.call-start = ((), (), s32[]{:S(2)}) async-start(), calls=%async_computation.2 | async-start | bytes 1310720 | tf_op jit(solution)/shard_map/all_gather | solution.py:99
  18.3 2.4 %copy-start.6 = (s32[1,8,256]{2,1,0:T(8,128)S(1)}, s32[1,8,256]{2,1,0:T(8,128)}, u32[]{:S(2)}) copy-start(s32[1,8,256]{2,1,0:T(8,128)} %param.9) | copy-start | bytes 24580
  20.8 8.6 %copy-start = (bf16[8,256,512]{2,1,0:T(8,128)(2,1)S(1)}, bf16[8,256,512]{2,1,0:T(8,128)(2,1)}, u32[]{:S(2)}) copy-start(bf16[8,256,512]{2,1,0:T(8,128)(2,1)} %param.7) | copy-start | bytes 6291460
  31.4 1.6 %copy-start.3 = (bf16[1,8,256,512]{2,3,1,0:T(8,128)(2,1)S(1)}, bf16[1,8,256,512]{2,3,1,0:T(8,128)(2,1)}, u32[]{:S(2)}) copy-start(bf16[1,8,256,512]{2,3,1,0:T(8,128)(2,1)} %copy.47) | copy-start | bytes 6291460
  34.6 1.6 %copy-start.4 = (bf16[8,256,512]{1,2,0:T(8,128)(2,1)}, bf16[8,256,512]{1,2,0:T(8,128)(2,1)S(1)}, u32[]{:S(2)}) copy-start(bf16[8,256,512]{1,2,0:T(8,128)(2,1)S(1)} %fusion.13) | copy-start | bytes 6291460
  67.2 12.5 %copy-start.1 = (f32[2,16,64,64]{3,2,1,0:T(8,128)S(1)}, f32[2,16,64,64]{3,2,1,0:T(8,128)}, u32[]{:S(2)}) copy-start(f32[2,16,64,64]{3,2,1,0:T(8,128)} %param.5) | copy-start | bytes 1572868
Sparse Core Ops, SparseCore 0:
  48.5 17.0 all-gather.2
